TPU v7x, 128 devices: a whole 4x4x4 slice. The times are simulated.
128 devices in a mesh: row: 4 (over x_lo, core), col: 32 (over y, z, x_hi).
Axes of the slice: x: 4 (x_hi: 2, x_lo: 2; x = x_hi * 2 + x_lo), y: 4, z: 4, core: 2. Of those that a mesh axis runs over, the one named last changes fastest.
Arguments:
- prompt_tokens: bfloat16 [32768, 2048], P('col', 'row'), may hold values from -6 to 6
- decode_tokens: bfloat16 [32, 2048], P('col', 'row'), may hold values from -6 to 6
- norm_gain: float32 [2048], replicated, may hold values from 0.25 to 1.75
- norm_bias: float32 [2048], replicated, may hold values from -3 to 3
- project_weight: float32 [2048, 6144], P(('row', 'col')), may hold values from -0.25 to 0.25
- dense_weight: float32 [2048, 2048], P(('row', 'col')), may hold values from -0.125 to 0.125
- expand_weight: float32 [2048, 8192], P(('row', 'col')), may hold values from -0.125 to 0.125
- reduce_weight: float32 [2048, 8192], P(('row', 'col')), may hold values from -0.0625 to 0.0625
- key_cache: bfloat16 [32, 32, 262144], P('col', 'row'), may hold values from -15 to 15
- value_cache: bfloat16 [32, 32, 262144], P('col', 'row'), may hold values from -12 to 12
- prompt_lengths: int32 [64], P('col'), may hold values from 128 to 512, as said below
- cache_ages: int32 [32], replicated, may hold values from 1 to 4096, as said below
- slot_request: int32 [32], replicated, may hold values from 0 to 31, each once
Outputs:
- prompt_out: bfloat16 [32768, 2048], P('col', 'row')
- decoded: bfloat16 [32, 2048], P('col', 'row')
Inputs may be any that keep to these rules, and one draw needn't show every extreme that they name: `prompt_lengths`: tokens of a prompt at or beyond its length are padding; some prompt is full in every draw. `cache_ages`: cached positions 0 to age - 1 of a request are valid and its new token stands at position age; some request has exactly 4096. `slot_request`: a permutation of the requests.
All inputs are finite; a program needn't handle non-finite values.
Results may differ from a plain program's by a relative error of at most 0.012.
The roundings to bfloat16 on the way count: a program that leaves them out, or rounds other values in their place, can miss the bound.
Values may be sent and summed in bfloat16 or wider, within the bound.
No kernel may reach another device: no remote copies, remote signals or barrier semaphores. Data moves between devices by JAX's collectives and lax.ppermute only.
A program may use at most 192 MiB of HBM per device.

v0:
```python
import jax
import jax.numpy as jnp
from jax import lax
from jax.sharding import PartitionSpec as P

HD = 64
ROT = 32
PLEN = 512
CTX = 4096
KEY_BLOCK = 512
NEG = -1e30


def layer_norm(rows, gain, bias):
    values = rows.astype(jnp.float32)
    centre = jnp.mean(values, axis=-1, keepdims=True)
    centred = values - centre
    deviation = jnp.mean(centred * centred, axis=-1, keepdims=True)
    return (centred * lax.rsqrt(deviation + 1e-05) * gain + bias).astype(jnp.bfloat16)


def rotary(vectors, position):
    half_width = ROT // 2
    frequency = 10000.0 ** (-2.0 * jnp.arange(half_width).astype(jnp.float32) / ROT)
    angle = position.astype(jnp.float32)[..., None, None] * frequency
    cosine = jnp.cos(angle)
    sine_value = jnp.sin(angle)
    lower_part = vectors[..., :half_width]
    upper_part = vectors[..., half_width:ROT]
    return jnp.concatenate(
        [
            lower_part * cosine - upper_part * sine_value,
            upper_part * cosine + lower_part * sine_value,
            vectors[..., ROT:],
        ],
        axis=-1,
    )


def restore_rows(block, row_count, col_count):
    width = block.shape[1]
    shard_rows = block.shape[0] // (row_count * col_count)
    return (
        block.reshape(col_count, row_count, shard_rows, width)
        .transpose(1, 0, 2, 3)
        .reshape(row_count * col_count * shard_rows, width)
    )


def on_device(
    prompt_tokens,
    decode_tokens,
    norm_gain,
    norm_bias,
    project_weight,
    dense_weight,
    expand_weight,
    reduce_weight,
    key_cache,
    value_cache,
    prompt_lengths,
    cache_ages,
    slot_request,
):
    half_float = jnp.bfloat16
    row_count = lax.axis_size("row")
    col_count = lax.axis_size("col")
    regrouped = (
        lax.all_to_all(
            project_weight.astype(half_float), "row", split_axis=1, concat_axis=0, tiled=True
        ),
        lax.all_to_all(
            dense_weight.astype(half_float), "row", split_axis=1, concat_axis=0, tiled=True
        ),
        lax.all_to_all(
            expand_weight.astype(half_float), "row", split_axis=1, concat_axis=0, tiled=True
        ),
        lax.all_to_all(
            reduce_weight.astype(half_float), "row", split_axis=1, concat_axis=0, tiled=True
        ),
    )
    gathered = (
        lax.all_gather(regrouped[0], "col", axis=0, tiled=True),
        lax.all_gather(regrouped[1], "col", axis=0, tiled=True),
        lax.all_gather(regrouped[2], "col", axis=0, tiled=True),
        lax.all_gather(regrouped[3], "col", axis=0, tiled=True),
    )
    w_project, w_dense, w_expand, w_reduce = [
        restore_rows(piece, row_count, col_count) for piece in gathered
    ]
    prompt_full, decode_full = (
        lax.all_gather(prompt_tokens, "row", axis=1, tiled=True),
        lax.all_gather(decode_tokens, "row", axis=1, tiled=True),
    )
    rows_prompt = prompt_full.shape[0]
    slot_local = decode_full.shape[0]
    prompt_count = rows_prompt // PLEN
    heads_local = w_dense.shape[1] // HD
    total_slots = slot_request.shape[0]
    scale = HD ** (-0.5)
    joined = jnp.concatenate([prompt_full, decode_full], axis=0)
    normed = layer_norm(joined, norm_gain, norm_bias)
    merged = jnp.dot(normed, w_project, preferred_element_type=jnp.float32)
    hidden = jax.nn.gelu(
        jnp.dot(normed, w_expand, preferred_element_type=jnp.float32), approximate=True
    ).astype(half_float)
    mlp_part = lax.dot_general(
        hidden, w_reduce, (((1,), (1,)), ((), ())), preferred_element_type=jnp.float32
    )
    places = jnp.arange(PLEN, dtype=jnp.int32)

    def prompt_block(items):
        block, length = items
        queries = rotary(block[:, :, 0], places).astype(half_float)
        keys_rot = rotary(block[:, :, 1], places).astype(half_float)
        values = block[:, :, 2].astype(half_float)
        scores = (
            jnp.einsum("qhd,khd->hqk", queries, keys_rot, preferred_element_type=jnp.float32)
            * scale
        )
        allowed = (places[None, :] <= places[:, None]) & (places[None, :] < length)
        scores = jnp.where(allowed[None], scores, NEG)
        top = jnp.max(scores, axis=-1, keepdims=True)
        raised = jnp.exp(scores - top)
        probs = (raised / jnp.sum(raised, axis=-1, keepdims=True)).astype(half_float)
        mixed = jnp.einsum("hqk,khd->qhd", probs, values, preferred_element_type=jnp.float32)
        return mixed.astype(half_float).reshape(PLEN, heads_local * HD)

    prompt_blocks = merged[:rows_prompt].reshape(prompt_count, PLEN, heads_local, 3, HD)
    prompt_mixed = lax.map(prompt_block, (prompt_blocks, prompt_lengths)).reshape(
        rows_prompt, heads_local * HD
    )
    col_index = lax.axis_index("col")
    first_slot = col_index * slot_local
    local_ids = first_slot + jnp.arange(slot_local, dtype=jnp.int32)
    own_request = lax.dynamic_slice_in_dim(slot_request, first_slot, slot_local)
    all_ids = jnp.arange(total_slots, dtype=jnp.int32)
    slot_match = own_request[:, None] == all_ids[None, :]
    slot_age = jnp.sum(jnp.where(slot_match, cache_ages[None, :], 0), axis=1)
    decode_pieces = merged[rows_prompt:].reshape(slot_local, heads_local, 3, HD)
    query_new = rotary(decode_pieces[:, :, 0], slot_age).astype(half_float)
    key_new = rotary(decode_pieces[:, :, 1], slot_age).astype(half_float)
    value_new = decode_pieces[:, :, 2].astype(half_float)
    packed = jnp.stack([query_new, key_new, value_new], axis=2).reshape(
        slot_local, heads_local * 3 * HD
    )
    handed = lax.all_gather(packed, "col", axis=0, tiled=True)
    chooser = (slot_request[None, :] == local_ids[:, None]).astype(half_float)
    mine = jnp.dot(chooser, handed, preferred_element_type=jnp.float32).astype(half_float)
    mine = mine.reshape(slot_local, heads_local, 3, HD)
    query = mine[:, :, 0]
    own_key = mine[:, :, 1]
    own_value = mine[:, :, 2]
    local_ages = lax.dynamic_slice_in_dim(cache_ages, first_slot, slot_local)
    keys_local = key_cache.reshape(slot_local, heads_local, CTX, HD)
    values_local = value_cache.reshape(slot_local, heads_local, CTX, HD)
    block_count = CTX // KEY_BLOCK

    def score_block(step, held):
        start = step * KEY_BLOCK
        keys_block = lax.dynamic_slice_in_dim(keys_local, start, KEY_BLOCK, 2)
        block_scores = (
            jnp.einsum("shd,shtd->sht", query, keys_block, preferred_element_type=jnp.float32)
            * scale
        )
        key_places = start + jnp.arange(KEY_BLOCK, dtype=jnp.int32)
        block_scores = jnp.where(
            key_places[None, None, :] < local_ages[:, None, None], block_scores, NEG
        )
        return lax.dynamic_update_slice_in_dim(held, block_scores, start, 2)

    cache_scores = lax.fori_loop(
        0, block_count, score_block, jnp.full((slot_local, heads_local, CTX), NEG, jnp.float32)
    )
    own_score = jnp.sum(query.astype(jnp.float32) * own_key.astype(jnp.float32), axis=-1) * scale
    decode_top = jnp.maximum(jnp.max(cache_scores, axis=-1), own_score)
    cache_raised = jnp.exp(cache_scores - decode_top[:, :, None])
    own_raised = jnp.exp(own_score - decode_top)
    decode_total = jnp.sum(cache_raised, axis=-1) + own_raised
    cache_probs = (cache_raised / decode_total[:, :, None]).astype(half_float)
    own_prob = (own_raised / decode_total).astype(half_float)

    def value_block(step, running):
        start = step * KEY_BLOCK
        probs_block = lax.dynamic_slice_in_dim(cache_probs, start, KEY_BLOCK, 2)
        values_block = lax.dynamic_slice_in_dim(values_local, start, KEY_BLOCK, 2)
        return running + jnp.einsum(
            "sht,shtd->shd", probs_block, values_block, preferred_element_type=jnp.float32
        )

    start_value = own_prob.astype(jnp.float32)[:, :, None] * own_value.astype(jnp.float32)
    decode_sum = lax.fori_loop(0, block_count, value_block, start_value)
    decode_mixed = decode_sum.astype(half_float).reshape(slot_local, heads_local * HD)
    returned = lax.all_gather(decode_mixed, "col", axis=0, tiled=True)
    picker = slot_match.astype(half_float)
    decode_heads = jnp.dot(picker, returned, preferred_element_type=jnp.float32).astype(half_float)
    mixed_all = jnp.concatenate([prompt_mixed, decode_heads], axis=0)
    attn_part = lax.dot_general(
        mixed_all, w_dense, (((1,), (1,)), ((), ())), preferred_element_type=jnp.float32
    )
    attn_prompt, attn_decode = (
        lax.psum_scatter(attn_part[:rows_prompt], "row", scatter_dimension=1, tiled=True),
        lax.psum_scatter(attn_part[rows_prompt:], "row", scatter_dimension=1, tiled=True),
    )
    mlp_prompt, mlp_decode = (
        lax.psum_scatter(
            mlp_part[:rows_prompt].astype(jnp.bfloat16), "row", scatter_dimension=1, tiled=True
        ).astype(jnp.float32),
        lax.psum_scatter(
            mlp_part[rows_prompt:].astype(jnp.bfloat16), "row", scatter_dimension=1, tiled=True
        ).astype(jnp.float32),
    )
    summed_prompt = attn_prompt + mlp_prompt
    summed_decode = attn_decode + mlp_decode
    prompt_result = prompt_tokens.astype(jnp.float32) + summed_prompt
    decode_result = decode_tokens.astype(jnp.float32) + summed_decode
    return (prompt_result.astype(half_float), decode_result.astype(half_float))


def solution(mesh):
    in_specs = (
        P("col", "row"),
        P("col", "row"),
        P(),
        P(),
        P(("row", "col"), None),
        P(("row", "col"), None),
        P(("row", "col"), None),
        P(("row", "col"), None),
        P("col", "row", None),
        P("col", "row", None),
        P("col"),
        P(),
        P(),
    )
    out_specs = (P("col", "row"), P("col", "row"))
    return jax.shard_map(
        on_device, mesh=mesh, in_specs=in_specs, out_specs=out_specs, check_vma=False
    )
```

profile of v0, /device:TPU:1, one launch (start us, length us, event | category | flops | bytes accessed | tf_op | source)
XLA Modules:
  0.0 743.6 jit_solution(17155492854786503554)
XLA Ops:
  8.1 7.7 %all_to_all.76 = bf16[16,4,512]{2,0,1:T(8,128)(2,1)} all-to-all(bf16[16,4,512]{2,0,1:T(8,128)(2,1)S(1)} %bitcast.183), channel_id=1, replica_groups=mesh['row'=4,'col'=32] {'row'}, dimensions={1} | all-to-all | bytes 131072 | tf_op jit(solution)/shard_map/all_to_all | solution.py:72
  17.7 8.5 %all_to_all.77 = bf16[16,4,1536]{2,0,1:T(8,128)(2,1)} all-to-all(bf16[16,4,1536]{2,0,1:T(8,128)(2,1)S(1)} %bitcast.177), channel_id=1, replica_groups=mesh['row'=4,'col'=32] {'row'}, dimensions={1} | all-to-all | bytes 393216 | tf_op jit(solution)/shard_map/all_to_all | solution.py:69
  27.4 8.8 %all_to_all.78 = bf16[16,4,2048]{2,0,1:T(8,128)(2,1)} all-to-all(bf16[16,4,2048]{2,0,1:T(8,128)(2,1)S(1)} %bitcast.175), channel_id=1, replica_groups=mesh['row'=4,'col'=32] {'row'}, dimensions={1} | all-to-all | bytes 524288 | tf_op jit(solution)/shard_map/all_to_all | solution.py:75
  47.6 6.1 reshape.576
  53.6 11.1 %reshape.545 = bf16[1,8,4096,64]{3,2,1,0:T(8,128)(2,1)} reshape(bf16[2097152]{0:T(1024)(128)(2,1)} %reshape.576) | data formatting | bytes 8388608 | tf_op jit(solution)/shard_map/reshape | solution.py:155
  64.7 6.0 reshape.578
  70.7 11.0 %reshape.546 = bf16[1,8,4096,64]{3,2,1,0:T(8,128)(2,1)} reshape(bf16[2097152]{0:T(1024)(128)(2,1)} %reshape.578) | data formatting | bytes 8388608 | tf_op jit(solution)/shard_map/reshape | solution.py:156
  81.8 5.1 all_gather.25
  91.4 44.8 %all-gather.8.cloned.1.call-done = bf16[1024,2048]{1,0:T(8,128)(2,1)} async-done(((bf16[1024,512]{1,0:T(8,128)(2,1)}), bf16[1024,2048]{1,0:T(8,128)(2,1)}) %all-gather.8.cloned.1.call-update) | async-done | bytes 4194320 | tf_op jit(solution)/shard_map/all_gather | solution.py:92
  142.2 89.1 %all-gather.10.cloned.1.call-done = bf16[2048,1536]{1,0:T(8,128)(2,1)} async-done(((bf16[64,1536]{1,0:T(8,128)(2,1)}), bf16[2048,1536]{1,0:T(8,128)(2,1)}) %all-gather.10.cloned.1.call-update) | async-done | bytes 6291472 | tf_op jit(solution)/shard_map/all_gather | solution.py:83
  235.2 7.0 fusion.85
  245.4 6.6 copy.77
  252.0 9.2 %reshape.540 = f32[2,512,8,3,64]{1,0,4,3,2:T(2,128)} reshape(f32[1024,1536]{0,1:T(8,128)} %copy.77) | data formatting | bytes 12582912 | tf_op jit(solution)/shard_map/reshape | solution.py:129
  261.7 79.5 %all-gather = bf16[32,1,1536]{2,1,0:T(2,128)(2,1)S(1)} all-gather(bf16[1,1,1536]{2,1,0:T(2,128)(2,1)S(1)} %reshape.556), channel_id=1, replica_groups=mesh['row'=4,'col'=32] {'col'}, dimensions={0}, use_global_device_ids=true | all-gather | bytes 101376 | tf_op jit(solution)/shard_map/all_gather | solution.py:147
  341.6 18.2 %while.40 = (s32[]{:T(128)}, f32[1,8,4096]{2,1,0:T(8,128)S(1)}, s32[1]{0:T(128)}, bf16[1,8,4096,64]{3,2,1,0:T(8,128)(2,1)}, bf16[1,8,64]{2,1,0:T(8,128)(2,1)S(1)...) while((s32[]{:T(128)}, f32[1,8,4096]{2,1,0:T(8,128)S(1)}, s32[1]{0:T(128)}, ...), condition=%wide.region_9.10_spmd, body=%wide.region_8.9_spmd.sunk | while | flops 533510 | bytes 1099931 | solution.py:172
  360.4 12.2 %while.41 = (s32[]{:T(128)}, f32[1,8,64]{2,1,0:T(8,128)S(1)}, bf16[1,8,4096]{2,1,0:T(8,128)(2,1)S(1)}, bf16[1,8,4096,64]{3,2,1,0:T(8,128)(2,1)}, s32[]{:T(128)}, /*index=5*/s32[]{:T(128)}, s32[]{:T(128)}, s32[]{:T(128)}) while((s32[]{:T(128)}, f32[1,8,64]{2,1,0:T(8,128)S(1)}, bf16[1,8,4096]{2,1,0:T(8,128)(2,1)S(1)}, ...), condition=%wide.region_13.14_spmd, body=%wide.region_12.13_spmd.sunk | while | flops 524806 | bytes 1081483 | solution.py:192
  372.8 75.5 %all-gather.1 = bf16[32,1,512]{2,1,0:T(2,128)(2,1)S(1)} all-gather(bf16[1,1,512]{2,1,0:T(2,128)(2,1)S(1)} %reshape.558), channel_id=1, replica_groups=mesh['row'=4,'col'=32] {'col'}, dimensions={0}, use_global_device_ids=true | all-gather | bytes 33792 | tf_op jit(solution)/shard_map/all_gather | solution.py:194
  449.5 53.5 %while.42 = (s32[]{:T(128)}, bf16[2,512,512]{2,1,0:T(8,128)(2,1)}, f32[2,512,8,3,64]{1,0,4,3,2:T(2,128)}, s32[2]{0:T(128)}, s32[]{:T(128)}) while((s32[]{:T(128)}, bf16[2,512,512]{2,1,0:T(8,128)(2,1)}, f32[2,512,8,3,64]{1,0,4,3,2:T(2,128)}, s32[2]{0:T(128)}, s32[]{:T(128)}) %tuple.118), condition=%wide.region_5.6_spmd.clone.clone, body=%wide.region_2.5_spmd.clone.clone.sunk | while | flops 554444288 | bytes 41063644 | solution.py:130
  451.7 6.1 constant_dynamic-slice_fusion.2
  460.8 8.3 %fusion.116 = (f32[8,512]{1,0:T(8,128)}, f32[8,512,512]{1,2,0:T(8,128)}) fusion(pred[512,512]{0,1:T(8,128)(4,1)S(1)} %fusion.115, bf16[512,8,32]{0,2,1:T(8,128)(2,1)} %slice.235, bf16[512,8,16]{0,2,1:T(8,128)(2,1)} %get-tuple-element.479, bf16[512,8,16]{0,2,1:T(8,128)(2,1)} %get-tuple-element.480, bf16[512,8,32]{0,2,1:T(8,128)(2,1)} %slice.236, ...), kind=kOutput, calls=%fused_computation.141.clone.1 | convolution fusion | flops 279970304 | bytes 9715712 | tf_op jit(solution)/shard_map/while/body/eval_jaxpr/sub | solution.py:124
  469.1 5.1 fusion.117
  478.4 6.1 constant_dynamic-slice_fusion.2
  487.6 8.3 %fusion.116 = (f32[8,512]{1,0:T(8,128)}, f32[8,512,512]{1,2,0:T(8,128)}) fusion(pred[512,512]{0,1:T(8,128)(4,1)S(1)} %fusion.115, bf16[512,8,32]{0,2,1:T(8,128)(2,1)} %slice.235, bf16[512,8,16]{0,2,1:T(8,128)(2,1)} %get-tuple-element.479, bf16[512,8,16]{0,2,1:T(8,128)(2,1)} %get-tuple-element.480, bf16[512,8,32]{0,2,1:T(8,128)(2,1)} %slice.236, ...), kind=kOutput, calls=%fused_computation.141.clone.1 | convolution fusion | flops 279970304 | bytes 9715712 | tf_op jit(solution)/shard_map/while/body/eval_jaxpr/sub | solution.py:124
  495.8 5.1 fusion.117
  512.3 8.4 %copy.91 = bf16[32,4,16,2048]{3,2,0,1:T(8,128)(2,1)} copy(bf16[32,4,16,2048]{3,2,1,0:T(8,128)(2,1)} %bitcast.161) | data formatting | bytes 16777216 | tf_op jit(solution)/shard_map/reshape | solution.py:44
  520.8 8.4 %copy.93 = bf16[32,4,16,2048]{3,2,0,1:T(8,128)(2,1)} copy(bf16[32,4,16,2048]{3,2,1,0:T(8,128)(2,1)} %bitcast.162) | data formatting | bytes 16777216 | tf_op jit(solution)/shard_map/reshape | solution.py:44
  529.2 27.6 %convolution_convert_fusion = bf16[1025,2048]{1,0:T(8,128)(2,1)} fusion(bf16[2048,2048]{1,0:T(8,128)(2,1)} %bitcast.164, bf16[2048,2048]{1,0:T(8,128)(2,1)} %bitcast.163, f32[2048]{0:T(1024)S(1)} %copy-done.9, f32[2048]{0:T(1024)S(1)} %copy-done.11, f32[1025]{0:T(1024)S(1)} %copy-done.5, f32[1025]{0:T(1024)S(1)} %broadcast_multiply_fusion, ...), kind=kOutput, calls=%fused_computation.73 | convolution fusion | flops 17236531200 | bytes 25198600 | tf_op jit(solution)/shard_map/dot_general | solution.py:107
  558.7 4.7 slice.170
  563.5 7.8 %slice.169 = f32[1024,2048]{1,0:T(8,128)} slice(f32[1025,2048]{1,0:T(8,128)} %copy-done.1), slice={[0:1024], [0:2048]} | slice | bytes 16777216 | tf_op jit(solution)/shard_map/slice | solution.py:202
  572.5 30.1 %reduce-scatter.15.cloned.1.call-done = bf16[512,1]{1,0:T(8,128)(2,1)} async-done(((bf16[2048,1]{1,0:T(8,128)(2,1)}), bf16[512,1]{1,0:T(8,128)(2,1)}) %reduce-scatter.15.cloned.1.call-update) | async-done | bytes 1040
  604.2 46.9 %reduce-scatter.11.cloned.1.call-done = bf16[1024,512]{1,0:T(8,128)(2,1)} async-done(((bf16[1024,2048]{1,0:T(8,128)(2,1)}), bf16[1024,512]{1,0:T(8,128)(2,1)}) %reduce-scatter.11.cloned.1.call-update) | async-done | bytes 1048592 | tf_op jit(solution)/shard_map/reduce_scatter | solution.py:206
  651.1 82.5 %reduce-scatter.9.cloned.1.call-done = f32[1024,512]{1,0:T(8,128)} async-done(((f32[1024,2048]{1,0:T(8,128)}), f32[1024,512]{1,0:T(8,128)}) %reduce-scatter.9.cloned.1.call-update) | async-done | bytes 2097168 | tf_op jit(solution)/shard_map/reduce_scatter | solution.py:202
  (186 shorter events, 97.0 us)
Async XLA Ops:
  7.2 81.1 %all-gather.12.cloned.1.call-start = ((), (), s32[]{:S(2)}) async-start(), calls=%async_computation.10 | async-start | bytes 2162688 | tf_op jit(solution)/shard_map/all_gather | solution.py:84
  15.9 120.4 %all-gather.8.cloned.1.call-start = ((), (), s32[]{:S(2)}) async-start(), calls=%async_computation.8 | async-start | bytes 5242880 | tf_op jit(solution)/shard_map/all_gather | solution.py:92
  16.6 214.6 %all-gather.10.cloned.1.call-start = ((), (), s32[]{:S(2)}) async-start(), calls=%async_computation.9 | async-start | bytes 6488064 | tf_op jit(solution)/shard_map/all_gather | solution.py:83
  26.3 486.1 %all-gather.14.cloned.1.call-start = ((), (), s32[]{:S(2)}) async-start(), calls=%async_computation.12 | async-start | bytes 8650752 | tf_op jit(solution)/shard_map/all_gather | solution.py:85
  38.0 48.9 %all-to-all-start.3 = ((bf16[16,4,2048]{2,0,1:T(8,128)(2,1)}), bf16[16,4,2048]{2,0,1:T(8,128)(2,1)S(1)}, u32[]{:S(2)}, u32[]{:S(2)}) async-start(bf16[16,4,2048]{2,0,1:T(8,128)(2,1)} %bitcast.126), calls=%async_computation.4 | async-start | bytes 524288 | tf_op jit(solution)/shard_map/all_to_all | solution.py:78
  42.5 478.3 %all-gather.16.cloned.1.call-start = ((), (), s32[]{:S(2)}) async-start(), calls=%async_computation.13 | async-start | bytes 8650752 | tf_op jit(solution)/shard_map/all_gather | solution.py:86
  64.7 17.1 %copy-start.6 = (bf16[1,512]{1,0:T(2,128)(2,1)S(1)}, bf16[1,512]{1,0:T(2,128)(2,1)}, u32[]{:S(2)}) copy-start(bf16[1,512]{1,0:T(2,128)(2,1)} %param.20) | copy-start | bytes 3076
  87.0 0.7 copy-start.3
  87.7 483.7 %reduce-scatter.13.cloned.1.call-start = ((), (), s32[]{:S(2)}) async-start(), calls=%async_computation.15 | async-start | bytes 1310720
  139.1 95.6 %copy-start.8 = (f32[2048]{0:T(1024)S(1)}, f32[2048]{0:T(1024)}, u32[]{:S(2)}) copy-start(f32[2048]{0:T(1024)} %param.22) | copy-start | bytes 24580
  139.1 95.6 %copy-start.10 = (f32[2048]{0:T(1024)S(1)}, f32[2048]{0:T(1024)}, u32[]{:S(2)}) copy-start(f32[2048]{0:T(1024)} %param.21) | copy-start | bytes 24580
  142.2 92.5 %copy-start.4 = (f32[1025]{0:T(1024)}, f32[1025]{0:T(1024)S(1)}, u32[]{:S(2)}) copy-start(f32[1025]{0:T(1024)S(1)} %add_rsqrt_fusion) | copy-start | bytes 12304
  231.2 4.0 copy-start
  252.0 89.2 %copy-start.12 = (s32[32]{0:T(128)S(1)}, s32[32]{0:T(128)}, u32[]{:S(2)}) copy-start(s32[32]{0:T(128)} %param.31) | copy-start | bytes 388
  507.3 3.3 copy-start.1
  512.1 90.5 %reduce-scatter.15.cloned.1.call-start = ((), (), s32[]{:S(2)}) async-start(), calls=%async_computation.16 | async-start | bytes 655360
  520.8 8.4 %copy-start.5 = (f32[1025]{0:T(1024)S(1)}, f32[1025]{0:T(1024)}, u32[]{:S(2)}) copy-start(f32[1025]{0:T(1024)} %copy-done.4) | copy-start | bytes 12304
  520.8 8.4 %copy-start.9 = (f32[2048]{0:T(1024)S(1)}, f32[2048]{0:T(1024)}, u32[]{:S(2)}) copy-start(f32[2048]{0:T(1024)} %param.22) | copy-start | bytes 24580
  520.8 8.4 %copy-start.11 = (f32[2048]{0:T(1024)S(1)}, f32[2048]{0:T(1024)}, u32[]{:S(2)}) copy-start(f32[2048]{0:T(1024)} %param.21) | copy-start | bytes 24580
  558.6 92.5 %reduce-scatter.11.cloned.1.call-start = ((), (), s32[]{:S(2)}) async-start(), calls=%async_computation.14 | async-start | bytes 5242880 | tf_op jit(solution)/shard_map/reduce_scatter | solution.py:206
  563.4 170.2 %reduce-scatter.9.cloned.1.call-start = ((), (), s32[]{:S(2)}) async-start(), calls=%async_computation.11 | async-start | bytes 10485760 | tf_op jit(solution)/shard_map/reduce_scatter | solution.py:202
  571.3 32.3 %copy-start.7 = (bf16[1,512]{1,0:T(2,128)(2,1)S(1)}, bf16[1,512]{1,0:T(2,128)(2,1)}, u32[]{:S(2)}) copy-start(bf16[1,512]{1,0:T(2,128)(2,1)} %param.20) | copy-start | bytes 3076
  571.3 162.3 %copy-start.2 = (bf16[1024,512]{1,0:T(8,128)(2,1)S(1)}, bf16[1024,512]{1,0:T(8,128)(2,1)}, u32[]{:S(2)}) copy-start(bf16[1024,512]{1,0:T(8,128)(2,1)} %param.19) | copy-start | bytes 3145732
Sparse Core Ops, SparseCore 0:
  16.0 71.9 all-gather.11
  89.6 46.5 all-gather.7
  139.2 91.9 all-gather.9
  234.2 104.1 all-gather.13
  341.4 102.0 all-gather.15
  512.2 45.2 reduce-scatter.12
  560.0 42.5 reduce-scatter.14
  605.1 45.9 reduce-scatter.10
  653.6 79.9 reduce-scatter.8
where the time goes:
time: 751 us; the launch traced here: 744 us
  waiting for transfers between devices  294 us (39%)
  blocking collectives  185 us (25%)
  local copies, waits for them, and re-layouts  127 us (17%)
  matrix products  91.1 us (12%)
  other arithmetic  25.6 us (3%)
  between operations  15 us (2%)
    all_gather x1, waiting for transfers between devices, on_device(): lax.all_gather(regrouped[0], 'col', axis=0, tiled=True)  89.1 us
    reduce_scatter x1, waiting for transfers between devices, on_device(): lax.psum_scatter(attn_part[:rows_prompt], 'row', scatter_dimension=1, til...  82.5 us
    all_gather x1, blocking collectives, on_device(): handed = lax.all_gather(packed, 'col', axis=0, tiled=True)  79.5 us
    all_gather x1, blocking collectives, on_device(): returned = lax.all_gather(decode_mixed, 'col', axis=0, tiled=True)  75.5 us
    reduce_scatter x1, waiting for transfers between devices, on_device(): lax.psum_scatter(mlp_part[:rows_prompt].astype(jnp.bfloat16), 'row', scat...  46.9 us
    all_gather x1, waiting for transfers between devices, on_device(): lax.all_gather(prompt_tokens, 'row', axis=1, tiled=True)  44.8 us
    unnamed x11, waiting for transfers between devices  30.9 us
    dot_general x1, matrix products, on_device(): lax.dot_general(hidden, w_reduce, (((1,), (1,)), ((), ())), preferred_ele...  27.6 us
  transfers between devices with their start and end apart: 10, of which 5 were waited for; matrix products, arithmetic and copies ran while one was open for 32% of the time, Pallas kernels for 0%

commit v1 on v0

--- a/solution.py
+++ b/solution.py
@@ -191,7 +191,15 @@
     start_value = own_prob.astype(jnp.float32)[:, :, None] * own_value.astype(jnp.float32)
     decode_sum = lax.fori_loop(0, block_count, value_block, start_value)
     decode_mixed = decode_sum.astype(half_float).reshape(slot_local, heads_local * HD)
-    returned = lax.all_gather(decode_mixed, "col", axis=0, tiled=True)
+    returned = jnp.concatenate(
+        lax.all_to_all(
+            jnp.stack([decode_mixed for _ in range(lax.axis_size("col"))], 0),
+            axis_name="col",
+            split_axis=0,
+            concat_axis=0,
+        ),
+        0,
+    )
     picker = slot_match.astype(half_float)
     decode_heads = jnp.dot(picker, returned, preferred_element_type=jnp.float32).astype(half_float)
     mixed_all = jnp.concatenate([prompt_mixed, decode_heads], axis=0)

time: 751 us -> 675 us (0.90)
  blocking collectives: 185 us -> 110 us
  waiting for transfers between devices: 294 us -> 286 us
    all_gather x1 -> x0, blocking collectives: 75.5 us -> none  [on_device(): returned = lax.all_gather(decode_mixed, 'col', axis=0, tiled=True)]
    unnamed x11, waiting for transfers between devices: 30.9 us -> 22.1 us
    unnamed x34 -> x35, local copies, waits for them, and re-layouts: 21.5 us -> 22.8 us
  transfers between devices with their start and end apart: 10 -> 11, of which waited for: 5 -> 5; matrix products, arithmetic and copies ran while one was open for 32% -> 36% of each run, Pallas kernels for 0% -> 0%
where the time goes in v1:
time: 675 us; the launch traced here: 668 us
  waiting for transfers between devices  286 us (42%)
  local copies, waits for them, and re-layouts  128 us (19%)
  blocking collectives  110 us (16%)
  matrix products  91.6 us (14%)
  other arithmetic  27 us (4%)
  between operations  14.9 us (2%)
  starting transfers between devices  9.66 us (1%)
    all_gather x1, waiting for transfers between devices, on_device(): lax.all_gather(regrouped[0], 'col', axis=0, tiled=True)  89.1 us
    reduce_scatter x1, waiting for transfers between devices, on_device(): lax.psum_scatter(attn_part[:rows_prompt], 'row', scatter_dimension=1, til...  82.5 us
    all_gather x1, blocking collectives, on_device(): handed = lax.all_gather(packed, 'col', axis=0, tiled=True)  79.5 us
    reduce_scatter x1, waiting for transfers between devices, on_device(): lax.psum_scatter(mlp_part[:rows_prompt].astype(jnp.bfloat16), 'row', scat...  47 us
    all_gather x1, waiting for transfers between devices, on_device(): lax.all_gather(prompt_tokens, 'row', axis=1, tiled=True)  44.8 us
    dot_general x1, matrix products, on_device(): lax.dot_general(hidden, w_reduce, (((1,), (1,)), ((), ())), preferred_ele...  27.6 us
    reshape x4, local copies, waits for them, and re-layouts, restore_rows(): block.reshape(col_count, row_count, shard_rows, width).transpose(1, 0, 2, 3)  23.4 us
    unnamed x35, local copies, waits for them, and re-layouts  22.8 us
  transfers between devices with their start and end apart: 11, of which 5 were waited for; matrix products, arithmetic and copies ran while one was open for 36% of the time, Pallas kernels for 0%

profile of v1, /device:TPU:1, one launch (start us, length us, event | category | flops | bytes accessed | tf_op | source)
XLA Modules:
  0.0 667.7 jit_solution(8969276921851607350)
XLA Ops:
  8.1 7.7 %all_to_all.81 = bf16[16,4,512]{2,0,1:T(8,128)(2,1)} all-to-all(bf16[16,4,512]{2,0,1:T(8,128)(2,1)S(1)} %bitcast.184), channel_id=1, replica_groups=mesh['row'=4,'col'=32] {'row'}, dimensions={1} | all-to-all | bytes 131072 | tf_op jit(solution)/shard_map/all_to_all | solution.py:72
  17.7 8.5 %all_to_all.82 = bf16[16,4,1536]{2,0,1:T(8,128)(2,1)} all-to-all(bf16[16,4,1536]{2,0,1:T(8,128)(2,1)S(1)} %bitcast.178), channel_id=1, replica_groups=mesh['row'=4,'col'=32] {'row'}, dimensions={1} | all-to-all | bytes 393216 | tf_op jit(solution)/shard_map/all_to_all | solution.py:69
  27.4 8.8 %all_to_all.83 = bf16[16,4,2048]{2,0,1:T(8,128)(2,1)} all-to-all(bf16[16,4,2048]{2,0,1:T(8,128)(2,1)S(1)} %bitcast.176), channel_id=1, replica_groups=mesh['row'=4,'col'=32] {'row'}, dimensions={1} | all-to-all | bytes 524288 | tf_op jit(solution)/shard_map/all_to_all | solution.py:75
  47.6 6.1 reshape.590
  53.7 11.1 %reshape.562 = bf16[1,8,4096,64]{3,2,1,0:T(8,128)(2,1)} reshape(bf16[2097152]{0:T(1024)(128)(2,1)} %reshape.590) | data formatting | bytes 8388608 | tf_op jit(solution)/shard_map/reshape | solution.py:155
  64.7 6.0 reshape.592
  70.8 11.1 %reshape.563 = bf16[1,8,4096,64]{3,2,1,0:T(8,128)(2,1)} reshape(bf16[2097152]{0:T(1024)(128)(2,1)} %reshape.592) | data formatting | bytes 8388608 | tf_op jit(solution)/shard_map/reshape | solution.py:156
  81.8 5.6 all_gather.22
  91.4 44.8 %all-gather.7.cloned.1.call-done = bf16[1024,2048]{1,0:T(8,128)(2,1)} async-done(((bf16[1024,512]{1,0:T(8,128)(2,1)}), bf16[1024,2048]{1,0:T(8,128)(2,1)}) %all-gather.7.cloned.1.call-update) | async-done | bytes 4194320 | tf_op jit(solution)/shard_map/all_gather | solution.py:92
  142.2 89.1 %all-gather.9.cloned.1.call-done = bf16[2048,1536]{1,0:T(8,128)(2,1)} async-done(((bf16[64,1536]{1,0:T(8,128)(2,1)}), bf16[2048,1536]{1,0:T(8,128)(2,1)}) %all-gather.9.cloned.1.call-update) | async-done | bytes 6291472 | tf_op jit(solution)/shard_map/all_gather | solution.py:83
  235.2 7.0 %fusion.85 = f32[1025,1536]{1,0:T(8,128)S(1)} fusion(bf16[2048,1536]{1,0:T(8,128)(2,1)S(1)} %bitcast.167, f32[2048]{0:T(1024)S(1)} %copy-done.8, f32[2048]{0:T(1024)S(1)} %copy-done.10, f32[1025]{0:T(1024)S(1)} %add_rsqrt_fusion, f32[1025]{0:T(1024)S(1)} %broadcast_multiply_fusion, bf16[1,2048]{1,0:T(2,128)(2,1)S(1)} %all_gather.22, ...), kind=kOutput, calls=%fused_computation.140 | convolution fusion | flops 6467635200 | bytes 16812040 | tf_op jit(solution)/shard_map/dot_general | solution.py:103
  245.4 6.6 copy.77
  252.0 9.2 %reshape.557 = f32[2,512,8,3,64]{1,0,4,3,2:T(2,128)} reshape(f32[1024,1536]{0,1:T(8,128)} %copy.77) | data formatting | bytes 12582912 | tf_op jit(solution)/shard_map/reshape | solution.py:129
  261.7 79.5 %all-gather = bf16[32,1,1536]{2,1,0:T(2,128)(2,1)S(1)} all-gather(bf16[1,1,1536]{2,1,0:T(2,128)(2,1)S(1)} %reshape.573), channel_id=1, replica_groups=mesh['row'=4,'col'=32] {'col'}, dimensions={0}, use_global_device_ids=true | all-gather | bytes 101376 | tf_op jit(solution)/shard_map/all_gather | solution.py:147
  341.6 18.7 %while.40 = (s32[]{:T(128)}, f32[1,8,4096]{2,1,0:T(8,128)S(1)}, s32[1]{0:T(128)}, bf16[1,8,4096,64]{3,2,1,0:T(8,128)(2,1)}, bf16[1,8,64]{2,1,0:T(8,128)(2,1)S(1)...) while((s32[]{:T(128)}, f32[1,8,4096]{2,1,0:T(8,128)S(1)}, s32[1]{0:T(128)}, ...), condition=%wide.region_9.10_spmd, body=%wide.region_8.9_spmd.sunk | while | flops 533510 | bytes 1099931 | solution.py:172
  360.9 12.1 %while.41 = (s32[]{:T(128)}, f32[1,8,64]{2,1,0:T(8,128)S(1)}, bf16[1,8,4096]{2,1,0:T(8,128)(2,1)S(1)}, bf16[1,8,4096,64]{3,2,1,0:T(8,128)(2,1)}, s32[]{:T(128)}, /*index=5*/s32[]{:T(128)}, s32[]{:T(128)}, s32[]{:T(128)}) while((s32[]{:T(128)}, f32[1,8,64]{2,1,0:T(8,128)S(1)}, bf16[1,8,4096]{2,1,0:T(8,128)(2,1)S(1)}, ...), condition=%wide.region_13.14_spmd, body=%wide.region_12.13_spmd.sunk | while | flops 524806 | bytes 1081483 | solution.py:192
  375.2 4.5 all-to-all-start.1
  380.0 54.2 %while.42 = (s32[]{:T(128)}, bf16[2,512,512]{2,1,0:T(8,128)(2,1)}, f32[2,512,8,3,64]{1,0,4,3,2:T(2,128)}, s32[2]{0:T(128)}, s32[]{:T(128)}) while((s32[]{:T(128)}, bf16[2,512,512]{2,1,0:T(8,128)(2,1)}, f32[2,512,8,3,64]{1,0,4,3,2:T(2,128)}, s32[2]{0:T(128)}, s32[]{:T(128)}) %tuple.118), condition=%wide.region_5.6_spmd.clone.clone, body=%wide.region_2.5_spmd.clone.clone.sunk | while | flops 554444288 | bytes 41063644 | solution.py:130
  382.3 6.2 constant_dynamic-slice_fusion.2
  391.6 8.6 %fusion.116 = (f32[8,512]{1,0:T(8,128)}, f32[8,512,512]{1,2,0:T(8,128)}) fusion(pred[512,512]{0,1:T(8,128)(4,1)S(1)} %fusion.115, bf16[512,8,32]{0,2,1:T(8,128)(2,1)} %slice.235, bf16[512,8,16]{0,2,1:T(8,128)(2,1)} %get-tuple-element.479, bf16[512,8,16]{0,2,1:T(8,128)(2,1)} %get-tuple-element.480, bf16[512,8,32]{0,2,1:T(8,128)(2,1)} %slice.236, ...), kind=kOutput, calls=%fused_computation.141.clone.1 | convolution fusion | flops 279970304 | bytes 9715712 | tf_op jit(solution)/shard_map/while/body/eval_jaxpr/sub | solution.py:124
  400.2 5.1 fusion.117
  409.6 6.1 constant_dynamic-slice_fusion.2
  418.8 8.3 %fusion.116 = (f32[8,512]{1,0:T(8,128)}, f32[8,512,512]{1,2,0:T(8,128)}) fusion(pred[512,512]{0,1:T(8,128)(4,1)S(1)} %fusion.115, bf16[512,8,32]{0,2,1:T(8,128)(2,1)} %slice.235, bf16[512,8,16]{0,2,1:T(8,128)(2,1)} %get-tuple-element.479, bf16[512,8,16]{0,2,1:T(8,128)(2,1)} %get-tuple-element.480, bf16[512,8,32]{0,2,1:T(8,128)(2,1)} %slice.236, ...), kind=kOutput, calls=%fused_computation.141.clone.1 | convolution fusion | flops 279970304 | bytes 9715712 | tf_op jit(solution)/shard_map/while/body/eval_jaxpr/sub | solution.py:124
  427.1 5.1 fusion.117
  445.1 8.4 %copy.91 = bf16[32,4,16,2048]{3,2,0,1:T(8,128)(2,1)} copy(bf16[32,4,16,2048]{3,2,1,0:T(8,128)(2,1)} %bitcast.162) | data formatting | bytes 16777216 | tf_op jit(solution)/shard_map/reshape | solution.py:44
  453.6 8.4 %copy.93 = bf16[32,4,16,2048]{3,2,0,1:T(8,128)(2,1)} copy(bf16[32,4,16,2048]{3,2,1,0:T(8,128)(2,1)} %bitcast.163) | data formatting | bytes 16777216 | tf_op jit(solution)/shard_map/reshape | solution.py:44
  461.9 27.6 %convolution_convert_fusion = bf16[1025,2048]{1,0:T(8,128)(2,1)} fusion(bf16[2048,2048]{1,0:T(8,128)(2,1)} %bitcast.165, bf16[2048,2048]{1,0:T(8,128)(2,1)} %bitcast.164, f32[2048]{0:T(1024)S(1)} %copy-done.9, f32[2048]{0:T(1024)S(1)} %copy-done.11, f32[1025]{0:T(1024)S(1)} %copy-done.5, f32[1025]{0:T(1024)S(1)} %broadcast_multiply_fusion, ...), kind=kOutput, calls=%fused_computation.73 | convolution fusion | flops 17236531200 | bytes 25198600 | tf_op jit(solution)/shard_map/dot_general | solution.py:107
  491.5 4.7 slice.170
  496.3 7.8 %slice.169 = f32[1024,2048]{1,0:T(8,128)} slice(f32[1025,2048]{1,0:T(8,128)} %copy-done.1), slice={[0:1024], [0:2048]} | slice | bytes 16777216 | tf_op jit(solution)/shard_map/slice | solution.py:210
  505.3 21.3 %reduce-scatter.15.cloned.1.call-done = bf16[512,1]{1,0:T(8,128)(2,1)} async-done(((bf16[2048,1]{1,0:T(8,128)(2,1)}), bf16[512,1]{1,0:T(8,128)(2,1)}) %reduce-scatter.15.cloned.1.call-update) | async-done | bytes 1040
  528.2 47.0 %reduce-scatter.11.cloned.1.call-done = bf16[1024,512]{1,0:T(8,128)(2,1)} async-done(((bf16[1024,2048]{1,0:T(8,128)(2,1)}), bf16[1024,512]{1,0:T(8,128)(2,1)}) %reduce-scatter.11.cloned.1.call-update) | async-done | bytes 1048592 | tf_op jit(solution)/shard_map/reduce_scatter | solution.py:214
  575.2 82.5 %reduce-scatter.9.cloned.1.call-done = f32[1024,512]{1,0:T(8,128)} async-done(((f32[1024,2048]{1,0:T(8,128)}), f32[1024,512]{1,0:T(8,128)}) %reduce-scatter.9.cloned.1.call-update) | async-done | bytes 2097168 | tf_op jit(solution)/shard_map/reduce_scatter | solution.py:210
  (192 shorter events, 99.8 us)
Async XLA Ops:
  7.2 81.0 %all-gather.11.cloned.1.call-start = ((), (), s32[]{:S(2)}) async-start(), calls=%async_computation.11 | async-start | bytes 2162688 | tf_op jit(solution)/shard_map/all_gather | solution.py:84
  15.9 120.4 %all-gather.7.cloned.1.call-start = ((), (), s32[]{:S(2)}) async-start(), calls=%async_computation.9 | async-start | bytes 5242880 | tf_op jit(solution)/shard_map/all_gather | solution.py:92
  16.6 214.6 %all-gather.9.cloned.1.call-start = ((), (), s32[]{:S(2)}) async-start(), calls=%async_computation.10 | async-start | bytes 6488064 | tf_op jit(solution)/shard_map/all_gather | solution.py:83
  26.3 418.9 %all-gather.13.cloned.1.call-start = ((), (), s32[]{:S(2)}) async-start(), calls=%async_computation.13 | async-start | bytes 8650752 | tf_op jit(solution)/shard_map/all_gather | solution.py:85
  38.0 49.4 %all-to-all-start.4 = ((bf16[16,4,2048]{2,0,1:T(8,128)(2,1)}), bf16[16,4,2048]{2,0,1:T(8,128)(2,1)S(1)}, u32[]{:S(2)}, u32[]{:S(2)}) async-start(bf16[16,4,2048]{2,0,1:T(8,128)(2,1)} %bitcast.127), calls=%async_computation.5 | async-start | bytes 524288 | tf_op jit(solution)/shard_map/all_to_all | solution.py:78
  42.5 411.1 %all-gather.15.cloned.1.call-start = ((), (), s32[]{:S(2)}) async-start(), calls=%async_computation.14 | async-start | bytes 8650752 | tf_op jit(solution)/shard_map/all_gather | solution.py:86
  64.7 17.1 %copy-start.6 = (bf16[1,512]{1,0:T(2,128)(2,1)S(1)}, bf16[1,512]{1,0:T(2,128)(2,1)}, u32[]{:S(2)}) copy-start(bf16[1,512]{1,0:T(2,128)(2,1)} %param.20) | copy-start | bytes 3076
  87.5 0.7 copy-start.3
  139.1 95.6 %copy-start.8 = (f32[2048]{0:T(1024)S(1)}, f32[2048]{0:T(1024)}, u32[]{:S(2)}) copy-start(f32[2048]{0:T(1024)} %param.22) | copy-start | bytes 24580
  139.1 95.6 %copy-start.10 = (f32[2048]{0:T(1024)S(1)}, f32[2048]{0:T(1024)}, u32[]{:S(2)}) copy-start(f32[2048]{0:T(1024)} %param.21) | copy-start | bytes 24580
  142.1 92.5 %copy-start.4 = (f32[1025]{0:T(1024)}, f32[1025]{0:T(1024)S(1)}, u32[]{:S(2)}) copy-start(f32[1025]{0:T(1024)S(1)} %add_rsqrt_fusion) | copy-start | bytes 12304
  231.2 4.0 copy-start
  252.0 89.2 %copy-start.12 = (s32[32]{0:T(128)S(1)}, s32[32]{0:T(128)}, u32[]{:S(2)}) copy-start(s32[32]{0:T(128)} %param.31) | copy-start | bytes 388
  375.2 59.0 %all-to-all-start.1 = ((bf16[32,2,256]{2,1,0:T(2,128)(2,1)}), bf16[32,2,256]{2,1,0:T(2,128)(2,1)}, u32[]{:S(2)}, u32[]{:S(2)}) async-start(bf16[32,2,256]{2,1,0:T(2,128)(2,1)} %reshape.594), calls=%async_computation.1 | async-start | bytes 65536 | tf_op jit(solution)/shard_map/all_to_all | solution.py:195
  379.8 124.4 %reduce-scatter.13.cloned.1.call-start = ((), (), s32[]{:S(2)}) async-start(), calls=%async_computation.16 | async-start | bytes 1310720
  440.1 3.3 copy-start.1
  444.9 81.7 %reduce-scatter.15.cloned.1.call-start = ((), (), s32[]{:S(2)}) async-start(), calls=%async_computation.17 | async-start | bytes 655360
  453.6 8.4 %copy-start.5 = (f32[1025]{0:T(1024)S(1)}, f32[1025]{0:T(1024)}, u32[]{:S(2)}) copy-start(f32[1025]{0:T(1024)} %copy-done.4) | copy-start | bytes 12304
  453.6 8.4 %copy-start.9 = (f32[2048]{0:T(1024)S(1)}, f32[2048]{0:T(1024)}, u32[]{:S(2)}) copy-start(f32[2048]{0:T(1024)} %param.22) | copy-start | bytes 24580
  453.6 8.4 %copy-start.11 = (f32[2048]{0:T(1024)S(1)}, f32[2048]{0:T(1024)}, u32[]{:S(2)}) copy-start(f32[2048]{0:T(1024)} %param.21) | copy-start | bytes 24580
  491.4 83.8 %reduce-scatter.11.cloned.1.call-start = ((), (), s32[]{:S(2)}) async-start(), calls=%async_computation.15 | async-start | bytes 5242880 | tf_op jit(solution)/shard_map/reduce_scatter | solution.py:214
  496.2 161.5 %reduce-scatter.9.cloned.1.call-start = ((), (), s32[]{:S(2)}) async-start(), calls=%async_computation.12 | async-start | bytes 10485760 | tf_op jit(solution)/shard_map/reduce_scatter | solution.py:210
  504.1 23.5 %copy-start.7 = (bf16[1,512]{1,0:T(2,128)(2,1)S(1)}, bf16[1,512]{1,0:T(2,128)(2,1)}, u32[]{:S(2)}) copy-start(bf16[1,512]{1,0:T(2,128)(2,1)} %param.20) | copy-start | bytes 3076
  504.1 153.6 %copy-start.2 = (bf16[1024,512]{1,0:T(8,128)(2,1)S(1)}, bf16[1024,512]{1,0:T(8,128)(2,1)}, u32[]{:S(2)}) copy-start(bf16[1024,512]{1,0:T(8,128)(2,1)} %param.19) | copy-start | bytes 3145732
Sparse Core Ops, SparseCore 0:
  16.0 71.9 all-gather.10
  89.7 46.5 all-gather.6
  139.2 91.9 all-gather.8
  234.2 104.0 all-gather.12
  341.4 101.3 all-gather.14
  445.6 36.1 reduce-scatter.12
  491.6 34.9 reduce-scatter.14
  529.1 46.0 reduce-scatter.10
  577.7 79.9 reduce-scatter.8
